TPU v7x, 128 devices: a whole 4x4x4 slice. The times are simulated.
128 devices in a mesh: section: 2 (over core), seq: 4 (over x), tensor: 16 (over z, y).
Axes of the slice: x: 4, y: 4, z: 4, core: 2. Of those that a mesh axis runs over, the one named last changes fastest.
Arguments:
- queries: bfloat16 [2560, 8192], P(('section', 'seq'), 'tensor'), may hold values from -200 to 200
- neighbours: bfloat16 [10240, 8192], P(('section', 'seq', 'tensor')), may hold values from -6 to 6
- kv_weight: bfloat16 [2, 8192, 8192], P(None, None, 'tensor'), may hold values from -0.0625 to 0.0625
- out_weight: bfloat16 [8192, 8192], P('tensor'), may hold values from -0.5 to 0.5
- slot_map: int32 [40], replicated, may hold values from 0 to 39, as said below
Outputs:
- mixed: bfloat16 [2560, 8192], P(('section', 'seq', 'tensor'))
Inputs may be any that keep to these rules, and one draw needn't show every extreme that they name: `slot_map`: distinct numbers; slot s lies on encoder shard s // 5; at most 2 spans of one sequence shard map to one encoder shard, and that many do for some pair of shards.
All inputs are finite; a program needn't handle non-finite values.
Results may differ from a plain program's by a relative error of at most 0.013.
Values may be sent and summed in bfloat16 or wider, within the bound.
No kernel may reach another device: no remote copies, remote signals or barrier semaphores. Data moves between devices by JAX's collectives and lax.ppermute only.
A program may use at most 128 MiB of HBM per device.

v0:
```python
import math
import jax
import jax.numpy as jnp
from jax import lax
from jax.sharding import PartitionSpec as P

HD = 128
SPAN = 64
PEER = 2
CH_DEV = 5
CAPC = 5
KEYS = 256


def attend(query_block, key_values):
    scores = jnp.einsum(
        "bqhd,bkhd->bhqk", query_block, key_values[:, :, 0], preferred_element_type=jnp.float32
    )
    scores = scores * (1.0 / math.sqrt(HD))
    peak = jnp.max(scores, axis=-1, keepdims=True)
    expo = jnp.exp(scores - peak)
    weights = (expo / jnp.sum(expo, axis=-1, keepdims=True)).astype(jnp.bfloat16)
    result = jnp.einsum(
        "bhqk,bkhd->bqhd", weights, key_values[:, :, 1], preferred_element_type=jnp.float32
    )
    return result.astype(jnp.bfloat16)


def on_device(queries, neighbours, kv_weight, out_weight, slot_map):
    groups = lax.axis_size(("section", "seq"))
    group_index = lax.axis_index(("section", "seq"))
    heads_local = kv_weight.shape[2] // HD
    per_peer = PEER
    spans = slot_map.shape[0]
    row_block = lax.all_gather(neighbours, "tensor", axis=0, tiled=True)
    result = jnp.einsum("rd,kde->rke", row_block, kv_weight, preferred_element_type=jnp.float32)
    projected = result.astype(jnp.bfloat16).reshape(row_block.shape[0], 2 * kv_weight.shape[2])
    slot_values = projected.reshape(CAPC, KEYS, 2, heads_local, HD)
    span_ids = jnp.arange(spans, dtype=jnp.int32)
    owner_shard = slot_map // CAPC
    slot_index = slot_map % CAPC
    seq_owner = span_ids // CH_DEV
    earlier = (seq_owner[:, None] == seq_owner[None, :]) & (
        owner_shard[:, None] == owner_shard[None, :]
    )
    earlier = earlier & (span_ids[None, :] < span_ids[:, None])
    arrival = jnp.sum(earlier.astype(jnp.int32), axis=1)
    target_ids = jnp.arange(groups, dtype=jnp.int32)[:, None, None]
    place_ids = jnp.arange(per_peer, dtype=jnp.int32)[None, :, None]
    selection = (seq_owner[None, None, :] == target_ids) & (arrival[None, None, :] == place_ids)
    selection = selection & (owner_shard[None, None, :] == group_index)
    send_slot = jnp.sum(jnp.where(selection, slot_index[None, None, :], 0), axis=-1)
    occupied = jnp.any(selection, axis=-1)
    own_shards = lax.dynamic_slice_in_dim(owner_shard, group_index * CH_DEV, CH_DEV)
    own_arrival = lax.dynamic_slice_in_dim(arrival, group_index * CH_DEV, CH_DEV)
    own_place = own_shards * per_peer + own_arrival
    query_blocks = queries.reshape(CH_DEV, SPAN, heads_local, HD)
    local_pairs = jnp.where(
        occupied[:, :, None, None, None, None], slot_values[send_slot], jnp.zeros((), jnp.bfloat16)
    )
    received = lax.all_to_all(
        local_pairs, ("section", "seq"), split_axis=0, concat_axis=0, tiled=True
    )
    key_values = received.reshape(groups * per_peer, KEYS, 2, heads_local, HD)[own_place]
    attended = attend(query_blocks, key_values)
    attended_flat = attended.reshape(CH_DEV * SPAN, heads_local * HD)
    mixed = lax.psum_scatter(
        jnp.dot(attended_flat, out_weight, preferred_element_type=jnp.float32),
        "tensor",
        scatter_dimension=0,
        tiled=True,
    )
    return mixed.astype(jnp.bfloat16)


def solution(mesh):
    placed = (
        P(("section", "seq"), "tensor"),
        P(("section", "seq", "tensor"), None),
        P(None, None, "tensor"),
        P("tensor", None),
        P(),
    )
    return jax.shard_map(
        on_device,
        mesh=mesh,
        in_specs=placed,
        out_specs=P(("section", "seq", "tensor"), None),
        check_vma=False,
    )
```

profile of v0, /device:TPU:0, one launch (start us, length us, event | category | flops | bytes accessed | tf_op | source)
XLA Modules:
  0.0 552.6 jit_solution(7348434239065273170)
XLA Ops:
  6.5 0.7 all-gather.2.cloned.1.call-update
  7.3 0.7 broadcast_compare_fusion
  8.0 0.2 convert_reduce_fusion
  8.1 0.7 and_select_fusion
  8.8 0.1 select_reduce_fusion
  9.1 0.2 fusion.18
  9.3 0.1 copy.20
  9.4 135.4 %all-gather.2.cloned.1.call-done = bf16[1280,8192]{1,0:T(8,128)(2,1)} async-done(((bf16[80,8192]{1,0:T(8,128)(2,1)}), bf16[1280,8192]{1,0:T(8,128)(2,1)}) %all-gather.2.cloned.1.call-update) | async-done | bytes 20971536 | tf_op jit(solution)/shard_map/all_gather | solution.py:35
  144.8 28.1 %fusion.3 = bf16[1280,2,512]{2,0,1:T(8,128)(2,1)} fusion(bf16[2,8192,512]{2,1,0:T(8,128)(2,1)} %param.7, bf16[1280,8192]{1,0:T(8,128)(2,1)} %all-gather.2.cloned.1.call-done), kind=kOutput, calls=%fused_computation.6 | convolution fusion | flops 21476147200 | bytes 40370176 | tf_op jit(solution)/shard_map/rd,kde->rke/dot_general | solution.py:36
  172.8 3.5 reshape_reshape.3
  176.4 8.8 %gather_fusion = bf16[16,256,2,4,128]{4,3,1,2,0:T(4,128)(2,1)} fusion(bf16[5,256,2,4,128]{4,3,1,0,2:T(4,128)(2,1)S(1)} %reshape_reshape.3, s32[1024]{0:T(1024)S(1)} %pad_clamp_fusion.1), kind=kCustom, calls=%fused_computation | custom fusion | bytes 16777280 | tf_op jit(solution)/shard_map/gather | solution.py:59
  185.2 7.7 %copy_select_fusion = bf16[8,2,256,2,4,128]{5,2,4,3,1,0:T(8,128)(2,1)} fusion(bf16[8,2,256,2,4,128]{5,4,2,3,1,0:T(4,128)(2,1)} %bitcast.41, pred[8,2]{1,0:T(8,128)(4,1)S(1)} %copy.20), kind=kLoop, calls=%fused_computation.5 | loop fusion | flops 4194304 | bytes 16777232 | tf_op jit(solution)/shard_map/jit(_where)/select_n | solution.py:58
  192.9 5.4 all-to-all-start
  198.4 0.6 dynamic-slice
  199.7 92.3 %all-to-all-done = bf16[8,2,256,2,4,128]{5,2,4,3,1,0:T(8,128)(2,1)} async-done(((bf16[8,2,256,2,4,128]{5,2,4,3,1,0:T(8,128)(2,1)}), bf16[8,2,256,2,4,128]{5,2,4,3,1,0:T(8,128)(2,1)}, u32[]{:S(2)}, u32[]{:S(2)}) %all-to-all-start) | async-done | bytes 8388640 | tf_op jit(solution)/shard_map/all_to_all | solution.py:61
  292.0 4.4 gather_fusion.1
  296.4 0.6 fusion.8
  297.0 1.1 copy-done
  298.1 0.4 fusion.20
  298.5 4.0 fusion.11
  302.6 0.3 copy.26
  302.8 8.9 %fusion.13 = f32[320,8192]{1,0:T(8,128)} fusion(bf16[512,8192]{1,0:T(8,128)(2,1)} %param.8, bf16[40,8,4,128]{3,2,1,0:T(4,128)(2,1)S(1)} %bitcast.42), kind=kOutput, calls=%fused_computation.19 | convolution fusion | flops 2684354560 | bytes 19202048 | tf_op jit(solution)/shard_map/dot_general | solution.py:68
  311.8 232.1 %all-reduce.2 = bf16[320,8192]{1,0:T(8,128)(2,1)} all-reduce(f32[320,8192]{1,0:T(8,128)} %fusion.13), channel_id=2, replica_groups=mesh['section'=2,'seq'=4,'tensor'=16] {'tensor'}, use_global_device_ids=true, to_apply=%region_5.6.clone | all-reduce | flops 2621440 | bytes 15728640
  543.9 1.9 dynamic-slice_convert_fusion
  (16 shorter events, 0.4 us)
Async XLA Ops:
  6.5 138.2 %all-gather.2.cloned.1.call-start = ((), (), s32[]{:S(2)}) async-start(), calls=%async_computation.1 | async-start | bytes 22282240 | tf_op jit(solution)/shard_map/all_gather | solution.py:35
  192.9 5.4 copy-start.1
  192.9 5.5 copy-start.2
  192.9 99.1 %all-to-all-start = ((bf16[8,2,256,2,4,128]{5,2,4,3,1,0:T(8,128)(2,1)}), bf16[8,2,256,2,4,128]{5,2,4,3,1,0:T(8,128)(2,1)}, u32[]{:S(2)}, u32[]{:S(2)}) async-start(bf16[8,2,256,2,4,128]{5,2,4,3,1,0:T(8,128)(2,1)} %copy_select_fusion), calls=%async_computation | async-start | bytes 16777216 | tf_op jit(solution)/shard_map/all_to_all | solution.py:61
  297.0 1.1 copy-start
Sparse Core Ops, SparseCore 0:
  9.5 135.2 all-gather.1
where the time goes:
time: 553 us
  blocking collectives  232 us (42%)
  waiting for transfers between devices  228 us (41%)
  matrix products  41.6 us (8%)
  local copies, waits for them, and re-layouts  20.9 us (4%)
  between operations  14.2 us (3%)
  other arithmetic  10.1 us (2%)
    unnamed x1, blocking collectives  232 us
    all_gather x1, waiting for transfers between devices, on_device(): row_block = lax.all_gather(neighbours, 'tensor', axis=0, tiled=True)  135 us
    all_to_all x1, waiting for transfers between devices, on_device(): lax.all_to_all(local_pairs, ('section', 'seq'), split_axis=0, concat_axis...  92.3 us
    dot_general x1, matrix products, on_device(): jnp.einsum('rd,kde->rke', row_block, kv_weight, preferred_element_type=jn...  28.1 us
  transfers between devices with their start and end apart: 2, of which 2 were waited for; matrix products, arithmetic and copies ran while one was open for 1% of the time, Pallas kernels for 0%

commit v1 on v0

--- a/solution.py
+++ b/solution.py
@@ -32,7 +32,16 @@
     heads_local = kv_weight.shape[2] // HD
     per_peer = PEER
     spans = slot_map.shape[0]
-    row_block = lax.all_gather(neighbours, "tensor", axis=0, tiled=True)
+    ways = lax.axis_size("tensor")
+    up = [(d, (d + 1) % ways) for d in range(ways)]
+    down = [(d, (d - 1) % ways) for d in range(ways)]
+    earlier_2, later = ([neighbours], [neighbours])
+    for _ in range(ways // 2):
+        earlier_2.append(lax.ppermute(earlier_2[-1], "tensor", up))
+    for _ in range((ways - 1) // 2):
+        later.append(lax.ppermute(later[-1], "tensor", down))
+    line = jnp.concatenate([*earlier_2[::-1], *later[1:]], axis=0)
+    row_block = jnp.roll(line, (lax.axis_index("tensor") - ways // 2) * neighbours.shape[0], axis=0)
     result = jnp.einsum("rd,kde->rke", row_block, kv_weight, preferred_element_type=jnp.float32)
     projected = result.astype(jnp.bfloat16).reshape(row_block.shape[0], 2 * kv_weight.shape[2])
     slot_values = projected.reshape(CAPC, KEYS, 2, heads_local, HD)

time: 553 us -> 710 us (1.28)
  waiting for transfers between devices: 228 us -> 299 us
  local copies, waits for them, and re-layouts: 20.9 us -> 81 us
  starting transfers between devices: 5.35 us -> 46 us
  between operations: 14.2 us -> 0.87 us
    ppermute x0 -> x15, waiting for transfers between devices: none -> 207 us  [the longest x8 207 us: on_device(): earlier_2.append(lax.ppermute(earlier_2[-1], 'tensor', up))]
    all_gather x1 -> x0, waiting for transfers between devices: 135 us -> none  [on_device(): row_block = lax.all_gather(neighbours, 'tensor', axis=0, tiled=True)]
    unnamed x7 -> x76, local copies, waits for them, and re-layouts: 1.66 us -> 60.5 us
    ppermute x0 -> x15, starting transfers between devices: none -> 40.7 us  [the longest x7 39 us: on_device(): later.append(lax.ppermute(later[-1], 'tensor', down))]
  transfers between devices with their start and end apart: 2 -> 16, of which waited for: 2 -> 11; matrix products, arithmetic and copies ran while one was open for 1% -> 5% of each run, Pallas kernels for 0% -> 0%
where the time goes in v1:
time: 710 us; the launch traced here: 709 us
  waiting for transfers between devices  299 us (42%)
  blocking collectives  232 us (33%)
  local copies, waits for them, and re-layouts  81 us (11%)
  starting transfers between devices  46 us (6%)
  matrix products  39.8 us (6%)
  other arithmetic  10.2 us (1%)
    unnamed x1, blocking collectives  232 us
    ppermute x8, waiting for transfers between devices, on_device(): earlier_2.append(lax.ppermute(earlier_2[-1], 'tensor', up))  207 us
    all_to_all x1, waiting for transfers between devices, on_device(): lax.all_to_all(local_pairs, ('section', 'seq'), split_axis=0, concat_axis...  92.2 us
    unnamed x76, local copies, waits for them, and re-layouts  60.5 us
    ppermute x7, starting transfers between devices, on_device(): later.append(lax.ppermute(later[-1], 'tensor', down))  39 us
    dot_general x1, matrix products, on_device(): jnp.einsum('rd,kde->rke', row_block, kv_weight, preferred_element_type=jn...  26.2 us
  transfers between devices with their start and end apart: 16, of which 11 were waited for; matrix products, arithmetic and copies ran while one was open for 5% of the time, Pallas kernels for 0%

profile of v1, /device:TPU:0, one launch (start us, length us, event | category | flops | bytes accessed | tf_op | source)
XLA Modules:
  0.0 709.4 jit_solution(7534826758015195904)
XLA Ops:
  1.7 34.0 %collective-permute-done = bf16[80,8192]{1,0:T(8,128)(2,1)S(1)} collective-permute-done((bf16[80,8192]{1,0:T(8,128)(2,1)}, bf16[80,8192]{1,0:T(8,128)(2,1)S(1)}, u32[]{:S(2)}, u32[]{:S(2)}) %collective-permute-start) | collective-permute-done | bytes 1310752 | tf_op jit(solution)/shard_map/ppermute | solution.py:40
  35.7 5.3 collective-permute-start.8
  41.0 27.9 %collective-permute-done.1 = bf16[80,8192]{1,0:T(8,128)(2,1)S(1)} collective-permute-done((bf16[80,8192]{1,0:T(8,128)(2,1)S(1)}, bf16[80,8192]{1,0:T(8,128)(2,1)S(1)}, u32[]{:S(2)}, u32[]{:S(2)}) %collective-permute-start.1) | collective-permute-done | bytes 1310752 | tf_op jit(solution)/shard_map/ppermute | solution.py:40
  70.1 5.3 collective-permute-start.9
  75.4 25.9 %collective-permute-done.2 = bf16[80,8192]{1,0:T(8,128)(2,1)S(1)} collective-permute-done((bf16[80,8192]{1,0:T(8,128)(2,1)S(1)}, bf16[80,8192]{1,0:T(8,128)(2,1)S(1)}, u32[]{:S(2)}, u32[]{:S(2)}) %collective-permute-start.2) | collective-permute-done | bytes 1310752 | tf_op jit(solution)/shard_map/ppermute | solution.py:40
  101.8 5.8 collective-permute-start.10
  107.6 25.3 %collective-permute-done.3 = bf16[80,8192]{1,0:T(8,128)(2,1)S(1)} collective-permute-done((bf16[80,8192]{1,0:T(8,128)(2,1)S(1)}, bf16[80,8192]{1,0:T(8,128)(2,1)S(1)}, u32[]{:S(2)}, u32[]{:S(2)}) %collective-permute-start.3) | collective-permute-done | bytes 1310752 | tf_op jit(solution)/shard_map/ppermute | solution.py:40
  133.0 5.8 collective-permute-start.11
  138.8 24.7 %collective-permute-done.4 = bf16[80,8192]{1,0:T(8,128)(2,1)S(1)} collective-permute-done((bf16[80,8192]{1,0:T(8,128)(2,1)S(1)}, bf16[80,8192]{1,0:T(8,128)(2,1)S(1)}, u32[]{:S(2)}, u32[]{:S(2)}) %collective-permute-start.4) | collective-permute-done | bytes 1310752 | tf_op jit(solution)/shard_map/ppermute | solution.py:40
  163.6 5.8 collective-permute-start.12
  169.4 24.2 %collective-permute-done.5 = bf16[80,8192]{1,0:T(8,128)(2,1)} collective-permute-done((bf16[80,8192]{1,0:T(8,128)(2,1)S(1)}, bf16[80,8192]{1,0:T(8,128)(2,1)}, u32[]{:S(2)}, u32[]{:S(2)}) %collective-permute-start.5) | collective-permute-done | bytes 1310752 | tf_op jit(solution)/shard_map/ppermute | solution.py:40
  194.2 5.4 collective-permute-start.13
  199.6 23.2 %collective-permute-done.6 = bf16[80,8192]{1,0:T(8,128)(2,1)} collective-permute-done((bf16[80,8192]{1,0:T(8,128)(2,1)}, bf16[80,8192]{1,0:T(8,128)(2,1)}, u32[]{:S(2)}, u32[]{:S(2)}) %collective-permute-start.6) | collective-permute-done | bytes 1310752 | tf_op jit(solution)/shard_map/ppermute | solution.py:40
  224.3 5.6 collective-permute-start.14
  229.9 21.4 %collective-permute-done.7 = bf16[80,8192]{1,0:T(8,128)(2,1)} collective-permute-done((bf16[80,8192]{1,0:T(8,128)(2,1)}, bf16[80,8192]{1,0:T(8,128)(2,1)}, u32[]{:S(2)}, u32[]{:S(2)}) %collective-permute-start.7) | collective-permute-done | bytes 1310752 | tf_op jit(solution)/shard_map/ppermute | solution.py:40
  310.2 26.2 %fusion.4 = bf16[1280,2,512]{2,0,1:T(8,128)(2,1)} fusion(bf16[2,8192,512]{2,1,0:T(8,128)(2,1)S(1)} %bitcast.44, bf16[2560,8192]{1,0:T(8,128)(2,1)} %constant_dynamic-update-slice_fusion, s32[]{:T(128)S(6)} %select_n.69), kind=kOutput, calls=%fused_computation.7 | convolution fusion | flops 21476147200 | bytes 40370180 | tf_op jit(solution)/shard_map/rd,kde->rke/dot_general | solution.py:45
  339.9 8.8 %gather_fusion = bf16[16,256,2,4,128]{4,3,1,2,0:T(4,128)(2,1)} fusion(bf16[5,256,2,4,128]{4,3,1,0,2:T(4,128)(2,1)S(1)} %reshape_reshape.3, s32[1024]{0:T(1024)S(1)} %pad_clamp_fusion.1), kind=kCustom, calls=%fused_computation | custom fusion | bytes 16777280 | tf_op jit(solution)/shard_map/gather | solution.py:68
  348.7 7.8 %copy_select_fusion = bf16[8,2,256,2,4,128]{5,2,4,3,1,0:T(8,128)(2,1)} fusion(bf16[8,2,256,2,4,128]{5,4,2,3,1,0:T(4,128)(2,1)} %bitcast.41, pred[8,2]{1,0:T(8,128)(4,1)S(1)} %copy.20), kind=kLoop, calls=%fused_computation.6 | loop fusion | flops 4194304 | bytes 16777232 | tf_op jit(solution)/shard_map/jit(_where)/select_n | solution.py:67
  356.5 5.2 all-to-all-start
  363.2 92.2 %all-to-all-done = bf16[8,2,256,2,4,128]{5,2,4,3,1,0:T(8,128)(2,1)} async-done(((bf16[8,2,256,2,4,128]{5,2,4,3,1,0:T(8,128)(2,1)}), bf16[8,2,256,2,4,128]{5,2,4,3,1,0:T(8,128)(2,1)}, u32[]{:S(2)}, u32[]{:S(2)}) %all-to-all-start) | async-done | bytes 8388640 | tf_op jit(solution)/shard_map/all_to_all | solution.py:70
  455.4 4.4 gather_fusion.1
  461.9 4.1 fusion.12
  466.3 9.0 %fusion.14 = f32[320,8192]{1,0:T(8,128)} fusion(bf16[512,8192]{1,0:T(8,128)(2,1)} %param.8, bf16[40,8,4,128]{3,2,1,0:T(4,128)(2,1)S(1)} %bitcast.42), kind=kOutput, calls=%fused_computation.20 | convolution fusion | flops 2684354560 | bytes 19202048 | tf_op jit(solution)/shard_map/dot_general | solution.py:77
  475.2 232.2 %all-reduce.2 = bf16[320,8192]{1,0:T(8,128)(2,1)} all-reduce(f32[320,8192]{1,0:T(8,128)} %fusion.14), channel_id=2, replica_groups=mesh['section'=2,'seq'=4,'tensor'=16] {'tensor'}, use_global_device_ids=true, to_apply=%region_5.6.clone | all-reduce | flops 2621440 | bytes 15728640
  (114 shorter events, 73.0 us)
Async XLA Ops:
  0.0 269.9 %copy-start = (bf16[80,8192]{1,0:T(8,128)(2,1)S(1)}, bf16[80,8192]{1,0:T(8,128)(2,1)}, u32[]{:S(2)}) copy-start(bf16[80,8192]{1,0:T(8,128)(2,1)} %param.6) | copy-start | bytes 3932164
  0.0 35.7 %collective-permute-start = (bf16[80,8192]{1,0:T(8,128)(2,1)}, bf16[80,8192]{1,0:T(8,128)(2,1)S(1)}, u32[]{:S(2)}, u32[]{:S(2)}) collective-permute-start(bf16[80,8192]{1,0:T(8,128)(2,1)} %param.6), channel_id=1, source_target_pairs={{0,1},{1,2},{2,3},{3,4},{4,5},{5,6},{6,7},{7,8},{8,9},{9,10},{10,1... | collective-permute-start | bytes 3932168 | tf_op jit(solution)/shard_map/ppermute | solution.py:40
  35.7 33.3 %collective-permute-start.1 = (bf16[80,8192]{1,0:T(8,128)(2,1)S(1)}, bf16[80,8192]{1,0:T(8,128)(2,1)S(1)}, u32[]{:S(2)}, u32[]{:S(2)}) collective-permute-start(bf16[80,8192]{1,0:T(8,128)(2,1)S(1)} %collective-permute-done), channel_id=1, source_target_pairs={{0,1},{1,2},{2,3},{3,4},{4,5},{5,6},{6,7},{7,8},{8,9},{9,10},{10,1... | collective-permute-start | bytes 3932168 | tf_op jit(solution)/shard_map/ppermute | solution.py:40
  35.7 33.3 %collective-permute-start.8 = (bf16[80,8192]{1,0:T(8,128)(2,1)}, bf16[80,8192]{1,0:T(8,128)(2,1)S(1)}, u32[]{:S(2)}, u32[]{:S(2)}) collective-permute-start(bf16[80,8192]{1,0:T(8,128)(2,1)} %param.6), channel_id=1, source_target_pairs={{0,15},{1,0},{2,1},{3,2},{4,3},{5,4},{6,5},{7,6},{8,7},{9,8},{10,9... | collective-permute-start | bytes 3932168 | tf_op jit(solution)/shard_map/ppermute | solution.py:42
  68.9 32.8 %copy-start.3 = (bf16[80,8192]{1,0:T(8,128)(2,1)}, bf16[80,8192]{1,0:T(8,128)(2,1)S(1)}, u32[]{:S(2)}) copy-start(bf16[80,8192]{1,0:T(8,128)(2,1)S(1)} %collective-permute-done.1) | copy-start | bytes 3932164
  68.9 32.4 %collective-permute-start.2 = (bf16[80,8192]{1,0:T(8,128)(2,1)S(1)}, bf16[80,8192]{1,0:T(8,128)(2,1)S(1)}, u32[]{:S(2)}, u32[]{:S(2)}) collective-permute-start(bf16[80,8192]{1,0:T(8,128)(2,1)S(1)} %collective-permute-done.1), channel_id=1, source_target_pairs={{0,1},{1,2},{2,3},{3,4},{4,5},{5,6},{6,7},{7,8},{8,9},{9,10},{10,1... | collective-permute-start | bytes 3932168 | tf_op jit(solution)/shard_map/ppermute | solution.py:40
  70.1 31.6 %collective-permute-start.9 = (bf16[80,8192]{1,0:T(8,128)(2,1)S(1)}, bf16[80,8192]{1,0:T(8,128)(2,1)S(1)}, u32[]{:S(2)}, u32[]{:S(2)}) collective-permute-start(bf16[80,8192]{1,0:T(8,128)(2,1)S(1)} %collective-permute-done.8), channel_id=1, source_target_pairs={{0,15},{1,0},{2,1},{3,2},{4,3},{5,4},{6,5},{7,6},{8,7},{9,8},{10,9... | collective-permute-start | bytes 3932168 | tf_op jit(solution)/shard_map/ppermute | solution.py:42
  101.3 31.7 %copy-start.7 = (bf16[80,8192]{1,0:T(8,128)(2,1)}, bf16[80,8192]{1,0:T(8,128)(2,1)S(1)}, u32[]{:S(2)}) copy-start(bf16[80,8192]{1,0:T(8,128)(2,1)S(1)} %collective-permute-done.2) | copy-start | bytes 3932164
  101.3 31.5 %collective-permute-start.3 = (bf16[80,8192]{1,0:T(8,128)(2,1)S(1)}, bf16[80,8192]{1,0:T(8,128)(2,1)S(1)}, u32[]{:S(2)}, u32[]{:S(2)}) collective-permute-start(bf16[80,8192]{1,0:T(8,128)(2,1)S(1)} %collective-permute-done.2), channel_id=1, source_target_pairs={{0,1},{1,2},{2,3},{3,4},{4,5},{5,6},{6,7},{7,8},{8,9},{9,10},{10,1... | collective-permute-start | bytes 3932168 | tf_op jit(solution)/shard_map/ppermute | solution.py:40
  101.8 31.3 %collective-permute-start.10 = (bf16[80,8192]{1,0:T(8,128)(2,1)S(1)}, bf16[80,8192]{1,0:T(8,128)(2,1)S(1)}, u32[]{:S(2)}, u32[]{:S(2)}) collective-permute-start(bf16[80,8192]{1,0:T(8,128)(2,1)S(1)} %collective-permute-done.9), channel_id=1, source_target_pairs={{0,15},{1,0},{2,1},{3,2},{4,3},{5,4},{6,5},{7,6},{8,7},{9,8},{10,9... | collective-permute-start | bytes 3932168 | tf_op jit(solution)/shard_map/ppermute | solution.py:42
  132.9 30.7 %copy-start.11 = (bf16[80,8192]{1,0:T(8,128)(2,1)}, bf16[80,8192]{1,0:T(8,128)(2,1)S(1)}, u32[]{:S(2)}) copy-start(bf16[80,8192]{1,0:T(8,128)(2,1)S(1)} %collective-permute-done.3) | copy-start | bytes 3932164
  132.9 30.7 %collective-permute-start.4 = (bf16[80,8192]{1,0:T(8,128)(2,1)S(1)}, bf16[80,8192]{1,0:T(8,128)(2,1)S(1)}, u32[]{:S(2)}, u32[]{:S(2)}) collective-permute-start(bf16[80,8192]{1,0:T(8,128)(2,1)S(1)} %collective-permute-done.3), channel_id=1, source_target_pairs={{0,1},{1,2},{2,3},{3,4},{4,5},{5,6},{6,7},{7,8},{8,9},{9,10},{10,1... | collective-permute-start | bytes 3932168 | tf_op jit(solution)/shard_map/ppermute | solution.py:40
  133.0 30.6 %collective-permute-start.11 = (bf16[80,8192]{1,0:T(8,128)(2,1)S(1)}, bf16[80,8192]{1,0:T(8,128)(2,1)}, u32[]{:S(2)}, u32[]{:S(2)}) collective-permute-start(bf16[80,8192]{1,0:T(8,128)(2,1)S(1)} %collective-permute-done.10), channel_id=1, source_target_pairs={{0,15},{1,0},{2,1},{3,2},{4,3},{5,4},{6,5},{7,6},{8,7},{9,8},{10,9... | collective-permute-start | bytes 3932168 | tf_op jit(solution)/shard_map/ppermute | solution.py:42
  163.6 29.9 %collective-permute-start.5 = (bf16[80,8192]{1,0:T(8,128)(2,1)S(1)}, bf16[80,8192]{1,0:T(8,128)(2,1)}, u32[]{:S(2)}, u32[]{:S(2)}) collective-permute-start(bf16[80,8192]{1,0:T(8,128)(2,1)S(1)} %collective-permute-done.4), channel_id=1, source_target_pairs={{0,1},{1,2},{2,3},{3,4},{4,5},{5,6},{6,7},{7,8},{8,9},{9,10},{10,1... | collective-permute-start | bytes 3932168 | tf_op jit(solution)/shard_map/ppermute | solution.py:40
  163.6 30.6 %collective-permute-start.12 = (bf16[80,8192]{1,0:T(8,128)(2,1)}, bf16[80,8192]{1,0:T(8,128)(2,1)}, u32[]{:S(2)}, u32[]{:S(2)}) collective-permute-start(bf16[80,8192]{1,0:T(8,128)(2,1)} %collective-permute-done.11), channel_id=1, source_target_pairs={{0,15},{1,0},{2,1},{3,2},{4,3},{5,4},{6,5},{7,6},{8,7},{9,8},{10,9... | collective-permute-start | bytes 3932168 | tf_op jit(solution)/shard_map/ppermute | solution.py:42
  193.5 29.3 %collective-permute-start.6 = (bf16[80,8192]{1,0:T(8,128)(2,1)}, bf16[80,8192]{1,0:T(8,128)(2,1)}, u32[]{:S(2)}, u32[]{:S(2)}) collective-permute-start(bf16[80,8192]{1,0:T(8,128)(2,1)} %collective-permute-done.5), channel_id=1, source_target_pairs={{0,1},{1,2},{2,3},{3,4},{4,5},{5,6},{6,7},{7,8},{8,9},{9,10},{10,1... | collective-permute-start | bytes 3932168 | tf_op jit(solution)/shard_map/ppermute | solution.py:40
  194.2 30.1 %collective-permute-start.13 = (bf16[80,8192]{1,0:T(8,128)(2,1)}, bf16[80,8192]{1,0:T(8,128)(2,1)}, u32[]{:S(2)}, u32[]{:S(2)}) collective-permute-start(bf16[80,8192]{1,0:T(8,128)(2,1)} %collective-permute-done.12), channel_id=1, source_target_pairs={{0,15},{1,0},{2,1},{3,2},{4,3},{5,4},{6,5},{7,6},{8,7},{9,8},{10,9... | collective-permute-start | bytes 3932168 | tf_op jit(solution)/shard_map/ppermute | solution.py:42
  222.8 28.4 %collective-permute-start.7 = (bf16[80,8192]{1,0:T(8,128)(2,1)}, bf16[80,8192]{1,0:T(8,128)(2,1)}, u32[]{:S(2)}, u32[]{:S(2)}) collective-permute-start(bf16[80,8192]{1,0:T(8,128)(2,1)} %collective-permute-done.6), channel_id=1, source_target_pairs={{0,1},{1,2},{2,3},{3,4},{4,5},{5,6},{6,7},{7,8},{8,9},{9,10},{10,1... | collective-permute-start | bytes 3932168 | tf_op jit(solution)/shard_map/ppermute | solution.py:40
  224.3 46.8 %copy-start.2 = (bf16[80,8192]{1,0:T(8,128)(2,1)S(1)}, bf16[80,8192]{1,0:T(8,128)(2,1)}, u32[]{:S(2)}) copy-start(bf16[80,8192]{1,0:T(8,128)(2,1)} %copy-done.1) | copy-start | bytes 3932164
  224.3 48.0 %copy-start.6 = (bf16[80,8192]{1,0:T(8,128)(2,1)S(1)}, bf16[80,8192]{1,0:T(8,128)(2,1)}, u32[]{:S(2)}) copy-start(bf16[80,8192]{1,0:T(8,128)(2,1)} %copy-done.5) | copy-start | bytes 3932164
  224.3 49.2 %copy-start.10 = (bf16[80,8192]{1,0:T(8,128)(2,1)S(1)}, bf16[80,8192]{1,0:T(8,128)(2,1)}, u32[]{:S(2)}) copy-start(bf16[80,8192]{1,0:T(8,128)(2,1)} %copy-done.9) | copy-start | bytes 3932164
  224.3 57.8 %collective-permute-start.14 = (bf16[80,8192]{1,0:T(8,128)(2,1)}, bf16[80,8192]{1,0:T(8,128)(2,1)S(1)}, u32[]{:S(2)}, u32[]{:S(2)}) collective-permute-start(bf16[80,8192]{1,0:T(8,128)(2,1)} %collective-permute-done.13), channel_id=1, source_target_pairs={{0,15},{1,0},{2,1},{3,2},{4,3},{5,4},{6,5},{7,6},{8,7},{9,8},{10,9... | collective-permute-start | bytes 3932168 | tf_op jit(solution)/shard_map/ppermute | solution.py:42
  266.1 24.6 %copy-start.14 = (bf16[80,8192]{1,0:T(8,128)(2,1)S(1)}, bf16[80,8192]{1,0:T(8,128)(2,1)}, u32[]{:S(2)}) copy-start(bf16[80,8192]{1,0:T(8,128)(2,1)} %copy-done.13) | copy-start | bytes 3932164
  356.5 98.9 %all-to-all-start = ((bf16[8,2,256,2,4,128]{5,2,4,3,1,0:T(8,128)(2,1)}), bf16[8,2,256,2,4,128]{5,2,4,3,1,0:T(8,128)(2,1)}, u32[]{:S(2)}, u32[]{:S(2)}) async-start(bf16[8,2,256,2,4,128]{5,2,4,3,1,0:T(8,128)(2,1)} %copy_select_fusion), calls=%async_computation | async-start | bytes 16777216 | tf_op jit(solution)/shard_map/all_to_all | solution.py:70
  (14 other events, 172.0 us)
